TPU v7x, 256 devices: a whole 4x4x8 slice. The times are simulated.
256 devices in a mesh: keys: 32 (over x, y, core), vocab: 8 (over z).
Axes of the slice: x: 4, y: 4, z: 8, core: 2. Of those that a mesh axis runs over, the one named last changes fastest.
Arguments:
- hidden: bfloat16 [1024, 4096], P(('keys', 'vocab')), may hold values from -24 to 24
- queries: bfloat16 [1024, 1024], P(('keys', 'vocab')), may hold values from -24 to 24
- probes: int32 [1024, 64], P(('keys', 'vocab')), may hold values from 0 to 95, as said below
- counts: int32 [1024], P(('keys', 'vocab')), may hold values from 16 to 64
- block_slot: int32 [96], replicated, may hold values from 0 to 95, as said below
- key_store: bfloat16 [96, 512, 1024], P('keys'), may hold values from -7 to 7
- stored_next_tokens: int32 [96, 512], replicated, may hold values from 0 to 128255
- head_weight: bfloat16 [4096, 128256], P(None, ('keys', 'vocab'))
Outputs:
- mixed_logp: float32 [1024, 128256], P(('keys', 'vocab'))
Inputs may be any that keep to these rules, and one draw needn't show every extreme that they name: `probes`: the 64 ids of a row are distinct block ids; only the first counts of them are probed. At most 2 of a row's 64 ids map through block_slot to slots held by one keys index. `block_slot`: A permutation of the slots; slot s lies in the part of the key store held by keys index s // 3.
All inputs are finite; a program needn't handle non-finite values.
Results may differ from a plain program's by a relative error of at most 0.0003.
Values may be sent and summed in bfloat16 or wider, within the bound.
No kernel may reach another device: no remote copies, remote signals or barrier semaphores. Data moves between devices by JAX's collectives and lax.ppermute only.
A program may use at most 128 MiB of HBM per device.

v0:
```python
import math
import jax
import jax.numpy as jnp
from jax import lax
from jax.sharding import PartitionSpec as P

LAMBDA = 0.25
SMOOTH = 0.1


def joined(part, axis, combine):
    gathered = jax.tree.map(lambda a: lax.all_gather(a, axis), part)

    def take(source):
        return jax.tree.map(lambda a: lax.dynamic_index_in_dim(a, source, 0, False), gathered)

    return lax.fori_loop(
        1, lax.axis_size(axis), lambda source, state: combine(state, take(source)), take(0)
    )


def merge_totals(earlier, later):
    row_peak = jnp.maximum(earlier[0], later[0])
    combined = earlier[1] * jnp.exp(earlier[0] - row_peak) + later[1] * jnp.exp(later[0] - row_peak)
    return (row_peak, combined)


def pick_blocks(table, index_row):
    return table[index_row]


def shards(hidden, queries, probes, counts, block_slot, key_store, stored_next_tokens, head_weight):
    rows_dev = hidden.shape[0]
    piece_cols = head_weight.shape[1]
    local_blocks = key_store.shape[0]
    block_len = key_store.shape[1]
    key_width = key_store.shape[2]
    key_count = lax.axis_size("keys")
    vocab_count = lax.axis_size("vocab")
    probe_cap = probes.shape[1]
    logits = jnp.dot(
        lax.all_gather(hidden, ("keys", "vocab"), axis=0, tiled=True),
        head_weight,
        preferred_element_type=jnp.float32,
    )
    local_peak = jnp.max(logits, axis=1)
    local_sum = jnp.sum(jnp.exp(logits - local_peak[:, None]), axis=1)
    row_peak, row_sum = joined((local_peak, local_sum), ("keys", "vocab"), merge_totals)
    logits = logits - (row_peak + jnp.log(row_sum))[:, None]
    blocks = logits.reshape(key_count, vocab_count, rows_dev, 1, 1, piece_cols)
    arrived = lax.all_to_all(
        lax.all_to_all(blocks, "keys", split_axis=0, concat_axis=3, tiled=True),
        "vocab",
        split_axis=1,
        concat_axis=4,
        tiled=True,
    )
    whole_rows = arrived.reshape(rows_dev, key_count * vocab_count * piece_cols)
    group_queries = lax.all_gather(queries, "keys", axis=0, tiled=True)
    flat_keys = key_store.reshape(local_blocks * block_len, key_width)
    key_norms = jnp.sum(jnp.square(flat_keys.astype(jnp.float32)), axis=1)
    query_norms = jnp.sum(jnp.square(group_queries.astype(jnp.float32)), axis=1)
    inner_prod = lax.dot_general(
        group_queries, flat_keys, (((1,), (1,)), ((), ())), preferred_element_type=jnp.float32
    )
    score_scale = 0.5 / math.sqrt(key_width)
    scores = -(query_norms[:, None] + key_norms[None, :] - 2.0 * inner_prod) * score_scale
    slot_ids = block_slot[probes]
    outgoing = scores.reshape(key_count, rows_dev, local_blocks, block_len)
    incoming = lax.all_to_all(outgoing, "keys", split_axis=0, concat_axis=2, tiled=True)
    every_slot = incoming.reshape(rows_dev, key_count * local_blocks, block_len)
    chosen = jax.vmap(pick_blocks)(every_slot, slot_ids)
    live_mask = (jnp.arange(probe_cap, dtype=jnp.int32)[None, :] < counts[:, None])[:, :, None]
    best_score = jnp.max(jnp.where(live_mask, chosen, -jnp.inf), axis=(1, 2), keepdims=True)
    raised = jnp.where(live_mask, jnp.exp(chosen - best_score), 0.0)
    weights = raised / jnp.sum(raised, axis=(1, 2), keepdims=True)
    tokens = stored_next_tokens[slot_ids]
    row_ids = jnp.broadcast_to(jnp.arange(rows_dev, dtype=jnp.int32)[:, None, None], tokens.shape)
    vocab_size = whole_rows.shape[1]
    knn_mass = jnp.zeros((rows_dev, vocab_size), jnp.float32).at[row_ids, tokens].add(weights)
    return jnp.log(
        LAMBDA * (knn_mass + SMOOTH / vocab_size) / (1.0 + SMOOTH)
        + (1.0 - LAMBDA) * jnp.exp(whole_rows)
    )


def solution(mesh):
    placed = (
        P(("keys", "vocab"), None),
        P(("keys", "vocab"), None),
        P(("keys", "vocab"), None),
        P(("keys", "vocab")),
        P(),
        P("keys", None, None),
        P(),
        P(None, ("keys", "vocab")),
    )
    return jax.shard_map(
        shards, mesh=mesh, in_specs=placed, out_specs=P(("keys", "vocab"), None), check_vma=False
    )
```

profile of v0, /device:TPU:1, one launch (start us, length us, event | category | flops | bytes accessed | tf_op | source)
XLA Modules:
  0.0 1358.9 jit_solution(2815163394601035959)
XLA Ops:
  7.3 125.8 %all-gather.12.cloned.1.call-done = bf16[256,4,4096]{2,1,0:T(4,128)(2,1)} async-done(((bf16[1,4,4096]{2,1,0:T(4,128)(2,1)}), bf16[256,4,4096]{2,1,0:T(4,128)(2,1)}) %all-gather.12.cloned.1.call-update) | async-done | bytes 8388624 | tf_op jit(solution)/shard_map/all_gather | solution.py:42
  133.1 12.5 reshape.128
  145.6 10.5 fusion.7
  156.1 2.5 exponential_reduce_fusion
  159.4 27.1 %all-gather.2 = bf16[32,4,1024]{2,1,0:T(4,128)(2,1)} all-gather(bf16[1,4,1024]{2,1,0:T(4,128)(2,1)S(1)} %bitcast.55), channel_id=1, replica_groups=mesh['keys'=32,'vocab'=8] {'keys'}, dimensions={0}, use_global_device_ids=true | all-gather | bytes 270336 | tf_op jit(solution)/shard_map/all_gather | solution.py:59
  186.5 1.7 reshape.126
  188.9 1.1 multiply_reduce_fusion.2
  190.0 3.0 fusion.2
  193.0 1.7 reshape.77
  194.8 1.2 copy.18
  196.0 4.4 all-to-all-start
  200.4 59.7 %all-gather.10.cloned.1.call-done = f32[262144]{0:T(1024)} async-done(((f32[1024]{0:T(1024)}), f32[262144]{0:T(1024)}) %all-gather.10.cloned.1.call-update) | async-done | bytes 1048592 | tf_op jit(solution)/shard_map/all_gather | solution.py:12
  260.2 2.4 reshape.115
  262.6 103.3 %all-gather.8.cloned.1.call-done = f32[262144]{0:T(1024)} async-done(((f32[1024]{0:T(1024)}), f32[262144]{0:T(1024)}) %all-gather.8.cloned.1.call-update) | async-done | bytes 1048592 | tf_op jit(solution)/shard_map/all_gather | solution.py:12
  365.9 2.4 reshape.114
  368.3 211.2 %while.17 = (s32[]{:T(128)}, f32[1024]{0:T(1024)S(1)}, f32[1024]{0:T(1024)S(1)}, f32[256,1024]{1,0:T(8,128)}, f32[256,1024]{1,0:T(8,128)}, /*index=5*/s32[]{:T(128)}, s32[]{:T(128)}, s32[]{:T(128)}) while((s32[]{:T(128)}, f32[1024]{0:T(1024)S(1)}, f32[1024]{0:T(1024)S(1)}, f32[256,1024]{1,0:T(8,128)}, f32[256,1024]{1,0:T(8,128)}, ...), condition=%wide.region_8.9_spmd, body=%wide.region_7.8_spmd.sunk | while | flops 6149 | bytes 41091 | solution.py:17
  369.1 0.8 constant_dynamic-slice_fusion.3
  370.0 0.8 constant_dynamic-slice_fusion.3
  370.8 0.8 constant_dynamic-slice_fusion.3
  371.6 0.8 constant_dynamic-slice_fusion.3
  372.5 0.8 constant_dynamic-slice_fusion.3
  373.3 0.8 constant_dynamic-slice_fusion.3
  374.1 0.8 constant_dynamic-slice_fusion.3
  374.9 0.8 constant_dynamic-slice_fusion.3
  375.8 0.8 constant_dynamic-slice_fusion.3
  376.6 0.8 constant_dynamic-slice_fusion.3
  377.4 0.8 constant_dynamic-slice_fusion.3
  378.3 0.8 constant_dynamic-slice_fusion.3
  379.1 0.8 constant_dynamic-slice_fusion.3
  379.9 0.8 constant_dynamic-slice_fusion.3
  380.7 0.8 constant_dynamic-slice_fusion.3
  381.6 0.8 constant_dynamic-slice_fusion.3
  382.4 0.8 constant_dynamic-slice_fusion.3
  383.2 0.8 constant_dynamic-slice_fusion.3
  384.1 0.8 constant_dynamic-slice_fusion.3
  384.9 0.8 constant_dynamic-slice_fusion.3
  391.5 0.8 constant_dynamic-slice_fusion.3
  407.3 0.8 constant_dynamic-slice_fusion.3
  423.0 0.8 constant_dynamic-slice_fusion.3
  438.7 0.8 constant_dynamic-slice_fusion.3
  454.5 0.8 constant_dynamic-slice_fusion.3
  470.2 0.8 constant_dynamic-slice_fusion.3
  486.0 0.8 constant_dynamic-slice_fusion.3
  501.7 0.8 constant_dynamic-slice_fusion.3
  517.4 0.8 constant_dynamic-slice_fusion.3
  533.2 0.8 constant_dynamic-slice_fusion.3
  548.9 0.8 constant_dynamic-slice_fusion.3
  564.7 0.8 constant_dynamic-slice_fusion.3
  579.6 1.6 broadcast_subtract_fusion
  581.1 1.9 copy.20
  583.1 1.7 reshape.79
  584.8 7.3 all-to-all-start.1
  592.1 1.9 gather_fusion
  594.2 1.0 gather_fusion.1
  596.8 2.1 gather_fusion.2
  599.8 683.5 %scatter_custom_fusion = f32[513024]{0:T(1024)} fusion(s32[131072]{0:T(1024)S(1)} %bitcast.50, f32[131072]{0:T(1024)S(1)} %bitcast.51, f32[]{:T(128)} %constant.63.clone.1), kind=kCustom, calls=%fused_computation.21 | custom fusion | flops 131072 | bytes 2052100
  1283.2 3.3 copy.22
  1286.6 4.6 all-to-all-start.2
  1291.2 3.1 broadcast_multiply_fusion
  1294.2 3.8 reshape.85
  1298.1 44.8 %all-to-all-done.2 = f32[1,8,4,32,1,501]{5,2,3,4,0,1:T(4,128)S(1)} async-done(((f32[1,8,4,32,1,501]{5,2,3,4,0,1:T(4,128)}), f32[1,8,4,32,1,501]{5,2,3,4,0,1:T(4,128)S(1)}, u32[]{:S(2)}, u32[]{:S(2)}) %all-to-all-start.2) | async-done | bytes 2052128 | tf_op jit(solution)/shard_map/all_to_all | solution.py:51
  1343.5 1.2 copy.23
  1344.7 3.5 mul.57
  1348.2 4.2 add_log_fusion
  (534 shorter events, 184.4 us)
Async XLA Ops:
  6.5 587.7 %copy-start = (s32[96,512]{1,0:T(8,128)S(1)}, s32[96,512]{1,0:T(8,128)}, u32[]{:S(2)}) copy-start(s32[96,512]{1,0:T(8,128)} %param.16) | copy-start | bytes 589828
  6.5 126.5 %all-gather.12.cloned.1.call-start = ((), (), s32[]{:S(2)}) async-start(), calls=%async_computation.5 | async-start | bytes 8421376 | tf_op jit(solution)/shard_map/all_gather | solution.py:42
  7.3 252.9 %all-gather.10.cloned.1.call-start = ((), (), s32[]{:S(2)}) async-start(), calls=%async_computation.4 | async-start | bytes 1052672 | tf_op jit(solution)/shard_map/all_gather | solution.py:12
  145.6 42.6 %copy-start.2 = (bf16[3,512,1024]{2,1,0:T(8,128)(2,1)S(1)}, bf16[3,512,1024]{2,1,0:T(8,128)(2,1)}, u32[]{:S(2)}) copy-start(bf16[3,512,1024]{2,1,0:T(8,128)(2,1)} %param.15) | copy-start | bytes 9437188
  156.1 2.6 copy-start.4
  156.1 3.2 copy-start.5
  158.6 207.3 %all-gather.8.cloned.1.call-start = ((), (), s32[]{:S(2)}) async-start(), calls=%async_computation.3 | async-start | bytes 1052672 | tf_op jit(solution)/shard_map/all_gather | solution.py:12
  194.8 5.6 copy-start.6
  196.0 388.8 %all-to-all-start = ((f32[32,4,3,512]{3,1,2,0:T(4,128)}), f32[32,4,3,512]{3,1,2,0:T(4,128)S(1)}, u32[]{:S(2)}, u32[]{:S(2)}) async-start(f32[32,4,3,512]{3,1,2,0:T(4,128)} %copy.18), calls=%async_computation | async-start | bytes 1572864 | tf_op jit(solution)/shard_map/all_to_all | solution.py:70
  200.4 379.1 %copy-start.3 = (f32[1024,501]{0,1:T(8,128)S(1)}, f32[1024,501]{0,1:T(8,128)}, u32[]{:S(2)}) copy-start(f32[1024,501]{0,1:T(8,128)} %get-tuple-element.157) | copy-start | bytes 6156292
  260.2 108.2 %slice-start = ((f32[262144]{0:T(1024)}), f32[1024]{0:T(1024)S(1)}, s32[]{:S(2)}) async-start(f32[262144]{0:T(1024)} %all-gather.10.cloned.1.call-done), calls=%async_computation.6 | async-start | bytes 8192 | tf_op jit(solution)/shard_map/jit(dynamic_index_in_dim)/dynamic_slice | solution.py:15
  365.9 2.4 slice-start.1
  584.8 7.3 copy-start.1
  584.8 698.5 %all-to-all-start.1 = ((f32[32,8,4,1,1,501]{5,2,1,4,3,0:T(4,128)}), f32[32,8,4,1,1,501]{5,2,1,4,3,0:T(4,128)}, u32[]{:S(2)}, u32[]{:S(2)}) async-start(f32[32,8,4,1,1,501]{5,2,1,4,3,0:T(4,128)} %bitcast.10), calls=%async_computation.1 | async-start | bytes 4194304 | tf_op jit(solution)/shard_map/all_to_all | solution.py:52
  594.2 1.1 copy-start.8
  595.2 0.7 copy-start.7
  595.9 0.7 copy-start.9
  1286.6 56.2 %all-to-all-start.2 = ((f32[1,8,4,32,1,501]{5,2,3,4,0,1:T(4,128)}), f32[1,8,4,32,1,501]{5,2,3,4,0,1:T(4,128)S(1)}, u32[]{:S(2)}, u32[]{:S(2)}) async-start(f32[1,8,4,32,1,501]{5,2,3,4,0,1:T(4,128)} %copy.22), calls=%async_computation.2 | async-start | bytes 4194304 | tf_op jit(solution)/shard_map/all_to_all | solution.py:51
Sparse Core Ops, SparseCore 0:
  11.0 121.9 all-gather.11
  158.8 101.3 all-gather.9
  263.9 101.9 all-gather.7
where the time goes:
time: 1380 us; the launch traced here: 1360 us
  other arithmetic  701 us (51%)
  waiting for transfers between devices  335 us (24%)
  local copies, waits for them, and re-layouts  245 us (18%)
  blocking collectives  27.1 us (2%)
  starting transfers between devices  16.3 us (1%)
    unnamed x4, other arithmetic  684 us
    dynamic_slice x259, local copies, waits for them, and re-layouts, take(): lax.dynamic_index_in_dim(a, source, 0, False)  201 us
    all_gather x2, waiting for transfers between devices, joined(): gathered = jax.tree.map(lambda a: lax.all_gather(a, axis), part)  163 us
    all_gather x1, waiting for transfers between devices, shards(): lax.all_gather(hidden, ('keys', 'vocab'), axis=0, tiled=True)  126 us
    all_to_all x1, waiting for transfers between devices, shards(): lax.all_to_all(lax.all_to_all(blocks, 'keys', split_axis=0, concat_axis=3...  44.8 us
  transfers between devices with their start and end apart: 6, of which 4 were waited for; matrix products, arithmetic and copies ran while one was open for 68% of the time, Pallas kernels for 0%

commit v1 on v0

--- a/solution.py
+++ b/solution.py
@@ -39,7 +39,12 @@
     vocab_count = lax.axis_size("vocab")
     probe_cap = probes.shape[1]
     logits = jnp.dot(
-        lax.all_gather(hidden, ("keys", "vocab"), axis=0, tiled=True),
+        jnp.concatenate(
+            lax.all_to_all(
+                jnp.stack([hidden] * lax.axis_size(("keys", "vocab"))), ("keys", "vocab"), 0, 0
+            ),
+            axis=0,
+        ),
         head_weight,
         preferred_element_type=jnp.float32,
     )

time: 1380 us -> 1460 us (1.058)
  blocking collectives: 27.1 us -> 229 us
  waiting for transfers between devices: 335 us -> 209 us
    all_to_all x0 -> x1, blocking collectives: none -> 203 us  [shards(): lax.all_to_all(jnp.stack([hidden] * lax.axis_size(('keys', 'vocab'))), ('...]
    all_gather x1 -> x0, waiting for transfers between devices: 126 us -> none  [shards(): lax.all_gather(hidden, ('keys', 'vocab'), axis=0, tiled=True)]
  transfers between devices with their start and end apart: 6 -> 5, of which waited for: 4 -> 3; matrix products, arithmetic and copies ran while one was open for 68% -> 64% of each run, Pallas kernels for 0% -> 0%
where the time goes in v1:
time: 1460 us; the launch traced here: 1440 us
  other arithmetic  701 us (48%)
  local copies, waits for them, and re-layouts  253 us (17%)
  blocking collectives  229 us (16%)
  waiting for transfers between devices  209 us (14%)
  starting transfers between devices  16.5 us (1%)
    unnamed x4, other arithmetic  684 us
    all_to_all x1, blocking collectives, shards(): lax.all_to_all(jnp.stack([hidden] * lax.axis_size(('keys', 'vocab'))), ('...  203 us
    dynamic_slice x259, local copies, waits for them, and re-layouts, take(): lax.dynamic_index_in_dim(a, source, 0, False)  201 us
    all_gather x2, waiting for transfers between devices, joined(): gathered = jax.tree.map(lambda a: lax.all_gather(a, axis), part)  163 us
    all_to_all x1, waiting for transfers between devices, shards(): lax.all_to_all(lax.all_to_all(blocks, 'keys', split_axis=0, concat_axis=3...  44.8 us
  transfers between devices with their start and end apart: 5, of which 3 were waited for; matrix products, arithmetic and copies ran while one was open for 64% of the time, Pallas kernels for 0%

profile of v1, /device:TPU:1, one launch (start us, length us, event | category | flops | bytes accessed | tf_op | source)
XLA Modules:
  0.0 1443.1 jit_solution(10931042942016281216)
XLA Ops:
  6.5 8.3 stack.2
  14.8 203.3 %all_to_all.47 = bf16[256,4,4096]{2,1,0:T(4,128)(2,1)} all-to-all(bf16[256,4,4096]{2,1,0:T(4,128)(2,1)} %stack.2), channel_id=1, replica_groups=mesh['keys'=32,'vocab'=8] {'keys','vocab'}, dimensions={0} | all-to-all | bytes 16777216 | tf_op jit(solution)/shard_map/all_to_all | solution.py:43
  218.1 12.5 reshape.84
  230.6 10.5 fusion.7
  241.1 2.5 exponential_reduce_fusion
  244.3 25.3 %all-gather.2 = bf16[32,4,1024]{2,1,0:T(4,128)(2,1)} all-gather(bf16[1,4,1024]{2,1,0:T(4,128)(2,1)S(1)} %bitcast.53), channel_id=1, replica_groups=mesh['keys'=32,'vocab'=8] {'keys'}, dimensions={0}, use_global_device_ids=true | all-gather | bytes 270336 | tf_op jit(solution)/shard_map/all_gather | solution.py:64
  269.6 1.7 reshape.132
  272.1 1.1 multiply_reduce_fusion.2
  273.2 3.0 fusion.2
  276.2 1.7 reshape.82
  277.9 1.2 copy.18
  279.1 4.6 all-to-all-start
  283.8 60.2 %all-gather.8.cloned.1.call-done = f32[262144]{0:T(1024)} async-done(((f32[1024]{0:T(1024)}), f32[262144]{0:T(1024)}) %all-gather.8.cloned.1.call-update) | async-done | bytes 1048592 | tf_op jit(solution)/shard_map/all_gather | solution.py:12
  344.1 2.5 reshape.121
  346.5 103.3 %all-gather.6.cloned.1.call-done = f32[262144]{0:T(1024)} async-done(((f32[1024]{0:T(1024)}), f32[262144]{0:T(1024)}) %all-gather.6.cloned.1.call-update) | async-done | bytes 1048592 | tf_op jit(solution)/shard_map/all_gather | solution.py:12
  449.8 2.4 reshape.120
  452.2 211.2 %while.17 = (s32[]{:T(128)}, f32[1024]{0:T(1024)S(1)}, f32[1024]{0:T(1024)S(1)}, f32[256,1024]{1,0:T(8,128)}, f32[256,1024]{1,0:T(8,128)}, /*index=5*/s32[]{:T(128)}, s32[]{:T(128)}, s32[]{:T(128)}) while((s32[]{:T(128)}, f32[1024]{0:T(1024)S(1)}, f32[1024]{0:T(1024)S(1)}, f32[256,1024]{1,0:T(8,128)}, f32[256,1024]{1,0:T(8,128)}, ...), condition=%wide.region_8.9_spmd, body=%wide.region_7.8_spmd.sunk | while | flops 6149 | bytes 41091 | solution.py:17
  453.0 0.8 constant_dynamic-slice_fusion.3
  453.9 0.8 constant_dynamic-slice_fusion.3
  454.7 0.8 constant_dynamic-slice_fusion.3
  455.5 0.8 constant_dynamic-slice_fusion.3
  456.4 0.8 constant_dynamic-slice_fusion.3
  457.2 0.8 constant_dynamic-slice_fusion.3
  458.0 0.8 constant_dynamic-slice_fusion.3
  458.8 0.8 constant_dynamic-slice_fusion.3
  459.7 0.8 constant_dynamic-slice_fusion.3
  460.5 0.8 constant_dynamic-slice_fusion.3
  461.3 0.8 constant_dynamic-slice_fusion.3
  462.2 0.8 constant_dynamic-slice_fusion.3
  463.0 0.8 constant_dynamic-slice_fusion.3
  463.8 0.8 constant_dynamic-slice_fusion.3
  464.6 0.8 constant_dynamic-slice_fusion.3
  465.5 0.8 constant_dynamic-slice_fusion.3
  466.3 0.8 constant_dynamic-slice_fusion.3
  467.1 0.8 constant_dynamic-slice_fusion.3
  473.8 0.8 constant_dynamic-slice_fusion.3
  489.5 0.8 constant_dynamic-slice_fusion.3
  505.2 0.8 constant_dynamic-slice_fusion.3
  521.0 0.8 constant_dynamic-slice_fusion.3
  536.7 0.8 constant_dynamic-slice_fusion.3
  552.5 0.8 constant_dynamic-slice_fusion.3
  568.2 0.8 constant_dynamic-slice_fusion.3
  583.9 0.8 constant_dynamic-slice_fusion.3
  599.7 0.8 constant_dynamic-slice_fusion.3
  615.4 0.8 constant_dynamic-slice_fusion.3
  631.2 0.8 constant_dynamic-slice_fusion.3
  646.9 0.8 constant_dynamic-slice_fusion.3
  662.6 0.8 constant_dynamic-slice_fusion.3
  663.5 1.5 broadcast_subtract_fusion
  665.0 1.9 copy.20
  666.9 1.7 reshape.85
  668.7 7.2 all-to-all-start.2
  675.9 1.9 gather_fusion
  678.1 1.0 gather_fusion.1
  680.7 2.1 gather_fusion.2
  683.6 683.5 %scatter_custom_fusion = f32[513024]{0:T(1024)} fusion(s32[131072]{0:T(1024)S(1)} %bitcast.49, f32[131072]{0:T(1024)S(1)} %bitcast.50, f32[]{:T(128)} %constant.63.clone.1), kind=kCustom, calls=%fused_computation.21 | custom fusion | flops 131072 | bytes 2052100
  1367.1 3.3 copy.22
  1370.5 4.6 all-to-all-start.3
  1375.0 3.1 broadcast_multiply_fusion
  1378.1 3.9 reshape.91
  1382.0 44.8 %all-to-all-done.3 = f32[1,8,4,32,1,501]{5,2,3,4,0,1:T(4,128)S(1)} async-done(((f32[1,8,4,32,1,501]{5,2,3,4,0,1:T(4,128)}), f32[1,8,4,32,1,501]{5,2,3,4,0,1:T(4,128)S(1)}, u32[]{:S(2)}, u32[]{:S(2)}) %all-to-all-start.3) | async-done | bytes 2052128 | tf_op jit(solution)/shard_map/all_to_all | solution.py:56
  1427.3 1.2 copy.23
  1428.6 3.5 mul.57
  1432.1 4.2 add_log_fusion
  (533 shorter events, 184.4 us)
Async XLA Ops:
  6.5 671.6 %copy-start = (s32[96,512]{1,0:T(8,128)S(1)}, s32[96,512]{1,0:T(8,128)}, u32[]{:S(2)}) copy-start(s32[96,512]{1,0:T(8,128)} %param.16) | copy-start | bytes 589828
  6.5 337.5 %all-gather.8.cloned.1.call-start = ((), (), s32[]{:S(2)}) async-start(), calls=%async_computation.5 | async-start | bytes 1052672 | tf_op jit(solution)/shard_map/all_gather | solution.py:12
  230.6 40.8 %copy-start.2 = (bf16[3,512,1024]{2,1,0:T(8,128)(2,1)S(1)}, bf16[3,512,1024]{2,1,0:T(8,128)(2,1)}, u32[]{:S(2)}) copy-start(bf16[3,512,1024]{2,1,0:T(8,128)(2,1)} %param.15) | copy-start | bytes 9437188
  241.1 2.6 copy-start.4
  241.1 3.3 copy-start.5
  243.6 206.2 %all-gather.6.cloned.1.call-start = ((), (), s32[]{:S(2)}) async-start(), calls=%async_computation.4 | async-start | bytes 1052672 | tf_op jit(solution)/shard_map/all_gather | solution.py:12
  277.9 5.9 copy-start.6
  279.1 389.5 %all-to-all-start = ((f32[32,4,3,512]{3,1,2,0:T(4,128)}), f32[32,4,3,512]{3,1,2,0:T(4,128)S(1)}, u32[]{:S(2)}, u32[]{:S(2)}) async-start(f32[32,4,3,512]{3,1,2,0:T(4,128)} %copy.18), calls=%async_computation | async-start | bytes 1572864 | tf_op jit(solution)/shard_map/all_to_all | solution.py:75
  283.8 379.6 %copy-start.3 = (f32[1024,501]{0,1:T(8,128)S(1)}, f32[1024,501]{0,1:T(8,128)}, u32[]{:S(2)}) copy-start(f32[1024,501]{0,1:T(8,128)} %get-tuple-element.157) | copy-start | bytes 6156292
  344.1 108.2 %slice-start = ((f32[262144]{0:T(1024)}), f32[1024]{0:T(1024)S(1)}, s32[]{:S(2)}) async-start(f32[262144]{0:T(1024)} %all-gather.8.cloned.1.call-done), calls=%async_computation.6 | async-start | bytes 8192 | tf_op jit(solution)/shard_map/jit(dynamic_index_in_dim)/dynamic_slice | solution.py:15
  449.8 2.4 slice-start.1
  668.7 7.3 copy-start.1
  668.7 698.5 %all-to-all-start.2 = ((f32[32,8,4,1,1,501]{5,2,1,4,3,0:T(4,128)}), f32[32,8,4,1,1,501]{5,2,1,4,3,0:T(4,128)}, u32[]{:S(2)}, u32[]{:S(2)}) async-start(f32[32,8,4,1,1,501]{5,2,1,4,3,0:T(4,128)} %bitcast.9), calls=%async_computation.2 | async-start | bytes 4194304 | tf_op jit(solution)/shard_map/all_to_all | solution.py:57
  678.1 1.1 copy-start.8
  679.1 0.7 copy-start.7
  679.7 0.7 copy-start.9
  1370.5 56.2 %all-to-all-start.3 = ((f32[1,8,4,32,1,501]{5,2,3,4,0,1:T(4,128)}), f32[1,8,4,32,1,501]{5,2,3,4,0,1:T(4,128)S(1)}, u32[]{:S(2)}, u32[]{:S(2)}) async-start(f32[1,8,4,32,1,501]{5,2,3,4,0,1:T(4,128)} %copy.22), calls=%async_computation.3 | async-start | bytes 4194304 | tf_op jit(solution)/shard_map/all_to_all | solution.py:56
Sparse Core Ops, SparseCore 0:
  243.7 100.3 all-gather.7
  347.8 101.9 all-gather.5
